TPU v7x, 128 devices: a whole 4x4x4 slice. The times are simulated.
128 devices in a mesh: dp: 4 (over x_hi, core), mp: 32 (over z, x_lo, y).
Axes of the slice: x: 4 (x_hi: 2, x_lo: 2; x = x_hi * 2 + x_lo), y: 4, z: 4, core: 2. Of those that a mesh axis runs over, the one named last changes fastest.
Arguments:
- prompt_rows: bfloat16 [65536, 2048], P(('dp', 'mp')), may hold values from -6 to 6
- step_rows: bfloat16 [16, 2048], P('dp', 'mp'), may hold values from -6 to 6
- attn_gain: float32 [2048], replicated, may hold values from 0.1 to 1.9
- latent_gain: float32 [512], replicated, may hold values from 0.1 to 1.9
- joined_qkva: float32 [2048, 3648], P('dp', 'mp'), may hold values from -2.4748737 to 2.4748737
- kv_up: float32 [512, 4096], P('dp', 'mp'), may hold values from -0.25 to 0.25
- out_proj: float32 [2048, 2048], P('dp', 'mp'), may hold values from -1.5 to 1.5
- latent_cache: bfloat16 [256, 16, 576], P(('dp', 'mp')), may hold values from -6 to 6
- page_table: int32 [16, 8], P('dp'), may hold values from 0 to 63, as said below
- cached_lengths: int32 [16], P('dp'), may hold values from 1 to 127, as said below
Outputs:
- prompt_out: bfloat16 [65536, 2048], P(('dp', 'mp'))
- step_out: bfloat16 [16, 2048], P('dp', 'mp')
Inputs may be any that keep to these rules, and one draw needn't show every extreme that they name: `page_table`: row r lists the slots of r's 8 pages, numbered within the pool of r's index of dp; slot g lies on index g // 2 of mp. No slot is listed twice within one index of dp. `cached_lengths`: some request has 127 cached tokens and some has one.
All inputs are finite; a program needn't handle non-finite values.
Results may differ from a plain program's by a relative error of at most 0.015.
Values may be sent and summed in bfloat16 or wider, within the bound.
No kernel may reach another device: no remote copies, remote signals or barrier semaphores. Data moves between devices by JAX's collectives and lax.ppermute only.
A program may use at most 128 MiB of HBM per device.

v0:
```python
import math

import jax
import jax.numpy as jnp
from jax import lax
from jax.sharding import PartitionSpec as P

H = 16
DN = 128
DR = 64
DV = 128
LAT = 512
LEN = 512


NORM_EPS = 1e-06
ROPE_BASE = 50000.0
MASKED = -1e30


def merged(x, axis, combine):
    everything = jax.tree.map(
        lambda part, kind: lax.all_gather(part.astype(kind), axis),
        x,
        jax.tree.map(lambda a: jnp.bfloat16 if a.dtype == jnp.float32 else a.dtype, x),
    )

    def take(k):
        return jax.tree.map(lambda part, own: part[k].astype(own.dtype), everything, x)

    return lax.fori_loop(
        1, lax.axis_size(axis), lambda k, so_far: combine(so_far, take(k)), take(0)
    )


def rms_scale(values, scales):
    widened = values.astype(jnp.float32)
    mean_square = jnp.mean(widened * widened, axis=-1, keepdims=True)
    return widened * lax.rsqrt(mean_square + NORM_EPS) * scales


def rotate(values, positions):
    rot_width = values.shape[-1]
    half_width = rot_width // 2
    freq_steps = jnp.arange(half_width, dtype=jnp.float32)
    inv_freqs = jnp.exp(freq_steps * (-2.0 * math.log(ROPE_BASE) / rot_width))
    angles = positions.astype(jnp.float32)[:, None] * inv_freqs[None, :]
    angle_shape = (positions.shape[0],) + (1,) * (values.ndim - 2) + (half_width,)
    cosine = jnp.cos(angles).reshape(angle_shape)
    sine_part = jnp.sin(angles).reshape(angle_shape)
    lower_half = values[..., :half_width]
    upper_half = values[..., half_width:]
    return jnp.concatenate(
        [
            lower_half * cosine - upper_half * sine_part,
            upper_half * cosine + lower_half * sine_part,
        ],
        axis=-1,
    )


def queries_keys(projected, positions, latent_gain, up_heads):
    head_cols = H * (DN + DR)
    row_count = projected.shape[0]
    query_cols = projected[:, :head_cols].reshape(row_count, H, DN + DR)
    query_rot = rotate(query_cols[..., DN:].astype(jnp.float32), positions).astype(jnp.bfloat16)
    latent = rms_scale(projected[:, head_cols : head_cols + LAT], latent_gain).astype(jnp.bfloat16)
    key_rot = rotate(projected[:, head_cols + LAT :].astype(jnp.float32), positions).astype(
        jnp.bfloat16
    )
    query_lat = jnp.einsum(
        "rhn,lhn->rhl", query_cols[..., :DN], up_heads[..., :DN], preferred_element_type=jnp.float32
    ).astype(jnp.bfloat16)
    queries = jnp.concatenate([query_lat, query_rot], axis=-1)
    key_rows = jnp.concatenate([latent, key_rot], axis=-1)
    return (queries, key_rows)


def prompt_attention(queries, query_ids, all_keys, all_ids, score_scale):
    row_count = queries.shape[0]
    block_rows = min(row_count, 512)
    block_count = row_count // block_rows
    query_blocks = queries.reshape(block_count, block_rows, H, queries.shape[-1])
    id_blocks = query_ids.reshape(block_count, block_rows)
    latent_keys = all_keys[:, :LAT]

    def one_block(block_args):
        query_part, id_part = block_args
        scores = (
            jnp.einsum("qhc,kc->qhk", query_part, all_keys, preferred_element_type=jnp.float32)
            * score_scale
        )
        same_prompt = id_part[:, None] // LEN == all_ids[None, :] // LEN
        allowed = same_prompt & (all_ids[None, :] <= id_part[:, None])
        scores = jnp.where(allowed[:, None, :], scores, MASKED)
        peak_score = jnp.max(scores, axis=-1, keepdims=True)
        weights = jnp.where(allowed[:, None, :], jnp.exp(scores - peak_score), 0.0)
        weight_sum = jnp.sum(weights, axis=-1, keepdims=True)
        summed = jnp.einsum(
            "qhk,kl->qhl",
            weights.astype(jnp.bfloat16),
            latent_keys,
            preferred_element_type=jnp.float32,
        )
        return (summed / weight_sum).astype(jnp.bfloat16)

    return lax.map(one_block, (query_blocks, id_blocks)).reshape(row_count, H, LAT)


def page_attention(queries, latent_cache, page_table, cached_lengths, mp_index, score_scale):
    slot_count = latent_cache.shape[0]
    page_rows = latent_cache.shape[1]
    flat_cache = latent_cache.reshape(slot_count * page_rows, latent_cache.shape[2])
    slot_ids = mp_index * slot_count + jnp.arange(slot_count, dtype=jnp.int32)
    matches = page_table[:, :, None] == slot_ids[None, None, :]
    owned = jnp.any(matches, axis=1)
    page_numbers = jnp.arange(page_table.shape[1], dtype=jnp.int32)[None, :, None]
    page_index = jnp.sum(jnp.where(matches, page_numbers, 0), axis=1)
    key_position = (
        page_index[:, :, None] * page_rows + jnp.arange(page_rows, dtype=jnp.int32)[None, None, :]
    )
    allowed = owned[:, :, None] & (key_position < cached_lengths[:, None, None])
    allowed = allowed.reshape(page_table.shape[0], slot_count * page_rows)
    scores = (
        jnp.einsum("rhc,kc->rhk", queries, flat_cache, preferred_element_type=jnp.float32)
        * score_scale
    )
    scores = jnp.where(allowed[:, None, :], scores, MASKED)
    peak_score = jnp.max(scores, axis=-1)
    weights = jnp.where(allowed[:, None, :], jnp.exp(scores - peak_score[..., None]), 0.0)
    weight_sum = jnp.sum(weights, axis=-1)
    summed = jnp.einsum(
        "rhk,kl->rhl",
        weights.astype(jnp.bfloat16),
        flat_cache[:, :LAT],
        preferred_element_type=jnp.float32,
    )
    return (peak_score, weight_sum, summed)


def combine_partial(first_state, second_state):
    peak_score = jnp.maximum(first_state[0], second_state[0])
    first_factor = jnp.exp(first_state[0] - peak_score)
    second_factor = jnp.exp(second_state[0] - peak_score)
    weight_sum = first_state[1] * first_factor + second_state[1] * second_factor
    summed = first_state[2] * first_factor[..., None] + second_state[2] * second_factor[..., None]
    return (peak_score, weight_sum, summed)


def on_device(
    prompt_rows,
    step_rows,
    attn_gain,
    latent_gain,
    joined_qkva,
    kv_up,
    out_proj,
    latent_cache,
    page_table,
    cached_lengths,
):
    prompt_count = prompt_rows.shape[0]
    mp_index = lax.axis_index("mp")
    mp_size = lax.axis_size("mp")
    score_scale = (DN + DR) ** (-0.5)
    trainer = (
        joined_qkva.astype(jnp.bfloat16),
        kv_up.astype(jnp.bfloat16),
        out_proj.astype(jnp.bfloat16),
    )
    step_full = lax.all_gather(step_rows, "mp", axis=1, tiled=True)
    stacked = jnp.concatenate([prompt_rows, step_full], axis=0)
    normed = rms_scale(stacked, attn_gain).astype(jnp.bfloat16)
    prompt_ids = jnp.arange(prompt_count, dtype=jnp.int32)
    positions = jnp.concatenate([prompt_ids % LEN, cached_lengths], axis=0)
    served = (
        lax.all_to_all(trainer[0], "mp", split_axis=0, concat_axis=1, tiled=True),
        lax.all_to_all(trainer[1], "mp", split_axis=0, concat_axis=1, tiled=True),
        lax.all_to_all(trainer[2], "mp", split_axis=0, concat_axis=1, tiled=True),
    )
    inputs = normed
    projected = jnp.dot(
        inputs,
        lax.all_gather(served[0], ("dp", "mp"), axis=0, tiled=True),
        preferred_element_type=jnp.float32,
    )
    up_full = lax.all_gather(served[1], ("dp", "mp"), axis=0, tiled=True)
    up_heads = up_full.reshape(LAT, H, DN + DV)
    queries, key_rows = queries_keys(
        projected.astype(jnp.bfloat16), positions, latent_gain, up_heads
    )
    prompt_queries = queries[:prompt_count]
    prompt_key_rows = key_rows[:prompt_count]
    step_queries = queries[prompt_count:]
    step_keys = key_rows[prompt_count:]
    prompt_latent = prompt_attention(
        prompt_queries, prompt_ids, prompt_key_rows, prompt_ids, score_scale
    )
    partial_state = page_attention(
        step_queries, latent_cache, page_table, cached_lengths, mp_index, score_scale
    )
    peak_score, weight_sum, summed = merged(partial_state, "mp", combine_partial)
    own_score = (
        jnp.einsum("rhc,rc->rh", step_queries, step_keys, preferred_element_type=jnp.float32)
        * score_scale
    )
    new_peak = jnp.maximum(peak_score, own_score)
    old_factor = jnp.exp(peak_score - new_peak)
    own_weight = jnp.exp(own_score - new_peak)
    weight_sum = weight_sum * old_factor + own_weight
    own_latent = step_keys[:, :LAT].astype(jnp.float32)
    own_half = own_weight.astype(jnp.bfloat16).astype(jnp.float32)
    summed = summed * old_factor[..., None] + own_half[..., None] * own_latent[:, None, :]
    step_latent = (summed / weight_sum[..., None]).astype(jnp.bfloat16)
    latent_out = jnp.concatenate([prompt_latent, step_latent], axis=0)
    heads_out = jnp.einsum(
        "rhl,lhv->rhv", latent_out, up_heads[..., DN:], preferred_element_type=jnp.float32
    ).astype(jnp.bfloat16)
    heads_out = heads_out.reshape(latent_out.shape[0], H * DV)
    inputs = heads_out
    attended = jnp.dot(
        inputs,
        lax.all_gather(served[2], ("dp", "mp"), axis=0, tiled=True),
        preferred_element_type=jnp.float32,
    )
    attended = attended.astype(jnp.bfloat16)
    prompt_out = attended[:prompt_count]
    col_width = attended.shape[1] // mp_size
    step_out = lax.dynamic_slice_in_dim(attended[prompt_count:], mp_index * col_width, col_width, 1)
    return (prompt_out, step_out)


def solution(mesh):
    placed = (
        P(("dp", "mp"), None),
        P("dp", "mp"),
        P(),
        P(),
        P("dp", "mp"),
        P("dp", "mp"),
        P("dp", "mp"),
        P(("dp", "mp"), None, None),
        P("dp", None),
        P("dp"),
    )
    return jax.shard_map(
        on_device,
        mesh=mesh,
        in_specs=placed,
        out_specs=(P(("dp", "mp"), None), P("dp", "mp")),
        check_vma=False,
    )
```

profile of v0, /device:TPU:0, one launch (start us, length us, event | category | flops | bytes accessed | tf_op | source)
XLA Modules:
  0.0 1175.5 jit_solution(8233573797560646817)
XLA Ops:
  8.1 17.6 %all_to_all.57 = bf16[32,4,128]{2,1,0:T(4,128)(2,1)} all-to-all(bf16[32,4,128]{2,1,0:T(4,128)(2,1)S(1)} %bitcast.86), channel_id=1, replica_groups=mesh['dp'=4,'mp'=32] {'mp'}, dimensions={0} | all-to-all | bytes 65536 | tf_op jit(solution)/shard_map/all_to_all | solution.py:178
  25.7 1.1 copy.96
  26.8 12.0 %all_to_all.58 = bf16[32,16,114]{2,1,0:T(8,128)(2,1)S(1)} all-to-all(bf16[32,16,114]{2,1,0:T(8,128)(2,1)S(1)} %bitcast.82), channel_id=1, replica_groups=mesh['dp'=4,'mp'=32] {'mp'}, dimensions={0} | all-to-all | bytes 233472 | tf_op jit(solution)/shard_map/all_to_all | solution.py:177
  39.8 77.4 %all-gather.3 = bf16[32,64,4]{1,2,0:T(4,128)(2,1)S(1)} all-gather(bf16[1,64,4]{1,2,0:T(4,128)(2,1)} %bitcast.95), channel_id=1, replica_groups=mesh['dp'=4,'mp'=32] {'mp'}, dimensions={0}, use_global_device_ids=true | all-gather | bytes 16896 | tf_op jit(solution)/shard_map/all_gather | solution.py:171
  120.4 2.1 fusion.18
  123.3 203.8 %all-gather.18.cloned.1.call-done = bf16[128,4,4096]{2,1,0:T(4,128)(2,1)} async-done(((bf16[1,4,4096]{2,1,0:T(4,128)(2,1)}), bf16[128,4,4096]{2,1,0:T(4,128)(2,1)}) %all-gather.18.cloned.1.call-update) | async-done | bytes 4194320 | tf_op jit(solution)/shard_map/all_gather | solution.py:187
  327.1 7.7 reshape.302
  334.8 5.1 fusion.67
  339.9 316.5 %all-gather.12.cloned.1.call-done = bf16[2048,3648]{1,0:T(8,128)(2,1)} async-done(((bf16[16,3648]{1,0:T(8,128)(2,1)}), bf16[2048,3648]{1,0:T(8,128)(2,1)}) %all-gather.12.cloned.1.call-update) | async-done | bytes 14942224 | tf_op jit(solution)/shard_map/all_gather | solution.py:184
  656.4 15.9 %convolution_convert_fusion = bf16[516,3648]{0,1:T(8,128)(2,1)S(1)} fusion(bf16[2048,3648]{1,0:T(8,128)(2,1)} %all-gather.12.cloned.1.call-done, f32[2048]{0:T(1024)S(1)} %copy-done.11, f32[516]{0:T(1024)S(1)} %add_rsqrt_fusion.1, bf16[4,2048]{1,0:T(4,128)(2,1)S(1)} %bitcast.90, bf16[512,2048]{1,0:T(8,128)(2,1)S(1)} %copy-done.5), kind=kOutput, calls=%fused_computation.27 | convolution fusion | flops 7719458816 | bytes 20830736 | tf_op jit(solution)/shard_map/dot_general | solution.py:182
  672.6 1.1 slice_convert_fusion.1
  674.5 1.1 copy-done.3
  675.7 2.0 copy.132
  677.8 2.3 convert_element_type.171
  680.7 5.0 convert_bitcast_fusion
  685.7 1.4 subtract_convert_fusion
  687.2 1.9 copy-done
  692.3 7.9 all-to-all-start.2
  700.5 8.2 all-to-all-done.2
  709.7 1.3 fusion.31
  711.0 8.0 pad_maximum_fusion
  719.0 1.3 fusion.33
  720.5 10.6 fusion.5
  731.1 17.3 %fusion.69 = (f32[512,16]{0,1:T(8,128)S(1)}, bf16[512,16,512]{0,2,1:T(8,128)(2,1)}) fusion(f32[512,16,512]{0,2,1:T(8,128)} %fusion.5, pred[512,512]{0,1:T(8,128)(4,1)S(1)} %fusion.35), kind=kOutput, calls=%fused_computation.121 | output fusion | flops 33554944 | bytes 25460736 | tf_op jit(solution)/shard_map/while/body/eval_jaxpr/sub | solution.py:97
  748.4 10.3 divide_convert_fusion
  759.0 77.2 %all-gather.5 = bf16[32,4,16]{2,1,0:T(4,128)(2,1)S(1)} all-gather(bf16[1,4,16]{2,1,0:T(4,128)(2,1)S(1)} %convert_bitcast_fusion.3), channel_id=2, replica_groups=mesh['dp'=4,'mp'=32] {'mp'}, dimensions={0}, use_global_device_ids=true | all-gather | bytes 4224 | tf_op jit(solution)/shard_map/all_gather | solution.py:23
  836.3 75.5 %all-gather.6 = bf16[32,4,16]{2,1,0:T(4,128)(2,1)S(1)} all-gather(bf16[1,4,16]{2,1,0:T(4,128)(2,1)S(1)} %bitcast.93), channel_id=3, replica_groups=mesh['dp'=4,'mp'=32] {'mp'}, dimensions={0}, use_global_device_ids=true | all-gather | bytes 4224 | tf_op jit(solution)/shard_map/all_gather | solution.py:23
  912.8 30.7 %while.23 = (s32[]{:T(128)}, f32[4,16]{1,0:T(4,128)S(1)}, f32[4,16]{1,0:T(4,128)S(1)}, f32[4,16,512]{2,1,0:T(8,128)S(1)}, bf16[32,4,16]{2,1,0:T(4,128)(2,1)S(1)}...) while((s32[]{:T(128)}, f32[4,16]{1,0:T(4,128)S(1)}, ...), condition=%wide.region_9.10_spmd, body=%wide.region_8.9_spmd.sunk | while | flops 131589 | bytes 330135 | solution.py:31
  912.8 0.9 fusion.79
  913.8 0.9 fusion.79
  914.8 0.9 fusion.79
  915.8 0.9 fusion.79
  916.8 0.9 fusion.79
  919.8 0.9 fusion.79
  920.8 0.9 fusion.79
  923.7 0.9 fusion.79
  926.7 0.9 fusion.79
  930.7 0.9 fusion.79
  931.7 0.9 fusion.79
  932.6 0.9 fusion.79
  933.6 0.9 fusion.79
  934.6 0.9 fusion.79
  939.6 0.9 fusion.79
  942.6 0.9 fusion.79
  943.9 5.8 convert_bitcast_fusion.1
  951.0 207.9 %all-gather.14.cloned.1.call-done = bf16[2048,2048]{1,0:T(8,128)(2,1)} async-done(((bf16[16,2048]{1,0:T(8,128)(2,1)}), bf16[2048,2048]{1,0:T(8,128)(2,1)}) %all-gather.14.cloned.1.call-update) | async-done | bytes 8388624 | tf_op jit(solution)/shard_map/all_gather | solution.py:223
  1158.9 7.9 convolution_convert_fusion.1
  1166.8 1.5 slice.120
  (141 shorter events, 31.0 us)
Async XLA Ops:
  7.2 319.9 %all-gather.18.cloned.1.call-start = ((), (), s32[]{:S(2)}) async-start(), calls=%async_computation.6 | async-start | bytes 4227072 | tf_op jit(solution)/shard_map/all_gather | solution.py:187
  25.7 630.7 %all-gather.12.cloned.1.call-start = ((), (), s32[]{:S(2)}) async-start(), calls=%async_computation.3 | async-start | bytes 15323136 | tf_op jit(solution)/shard_map/all_gather | solution.py:184
  39.7 872.2 %all-gather.16.cloned.1.call-start = ((), (), s32[]{:S(2)}) async-start(), calls=%async_computation.5 | async-start | bytes 2162688 | tf_op jit(solution)/shard_map/all_gather | solution.py:23
  334.8 321.6 %copy-start.5 = (bf16[512,2048]{1,0:T(8,128)(2,1)S(1)}, bf16[512,2048]{1,0:T(8,128)(2,1)}, u32[]{:S(2)}) copy-start(bf16[512,2048]{1,0:T(8,128)(2,1)} %param.12) | copy-start | bytes 6291460
  334.8 321.6 %copy-start.11 = (f32[2048]{0:T(1024)S(1)}, f32[2048]{0:T(1024)}, u32[]{:S(2)}) copy-start(f32[2048]{0:T(1024)} %param.14) | copy-start | bytes 24580
  672.2 2.3 copy-start.4
  672.6 3.0 copy-start.3
  677.7 2.3 copy-start.7
  680.7 5.0 slice-start
  680.7 5.0 slice-start.1
  685.7 3.3 copy-start
  687.1 2.6 copy-start.1
  687.1 3.1 copy-start.2
  689.0 1.3 copy-start.9
  689.0 2.4 copy-start.8
  692.3 16.4 %all-to-all-start.2 = ((bf16[32,2,512]{2,1,0:T(2,128)(2,1)}), bf16[32,2,512]{2,1,0:T(2,128)(2,1)S(1)}, u32[]{:S(2)}, u32[]{:S(2)}) async-start(bf16[32,2,512]{2,1,0:T(2,128)(2,1)} %reshape.345), calls=%async_computation.2 | async-start | bytes 131072 | tf_op jit(solution)/shard_map/all_to_all | solution.py:179
  700.2 458.7 %all-gather.14.cloned.1.call-start = ((), (), s32[]{:S(2)}) async-start(), calls=%async_computation.4 | async-start | bytes 8454144 | tf_op jit(solution)/shard_map/all_gather | solution.py:223
  711.0 8.0 copy-start.10
  748.4 195.6 %copy-start.6 = (bf16[512,16,128]{2,1,0:T(8,128)(2,1)S(1)}, bf16[512,16,128]{2,1,0:T(8,128)(2,1)}, u32[]{:S(2)}) copy-start(bf16[512,16,128]{2,1,0:T(8,128)(2,1)} %get-tuple-element.225) | copy-start | bytes 6291460
Sparse Core Ops, SparseCore 0:
  25.8 301.2 all-gather.17
  328.8 327.5 all-gather.11
  691.5 154.5 all-gather.15
  847.6 311.1 all-gather.13
where the time goes:
time: 1180 us
  waiting for transfers between devices  737 us (62%)
  blocking collectives  260 us (22%)
  other arithmetic  70.6 us (6%)
  matrix products  56.7 us (5%)
  local copies, waits for them, and re-layouts  28.9 us (2%)
  between operations  14.2 us (1%)
    all_gather x1, waiting for transfers between devices, on_device(): lax.all_gather(served[0], ('dp', 'mp'), axis=0, tiled=True)  316 us
    all_gather x1, waiting for transfers between devices, on_device(): lax.all_gather(served[2], ('dp', 'mp'), axis=0, tiled=True)  208 us
    all_gather x1, waiting for transfers between devices, on_device(): up_full = lax.all_gather(served[1], ('dp', 'mp'), axis=0, tiled=True)  204 us
    all_gather x2, blocking collectives, merged(): lax.all_gather(part.astype(kind), axis)  153 us
    all_gather x1, blocking collectives, on_device(): step_full = lax.all_gather(step_rows, 'mp', axis=1, tiled=True)  77.4 us
    add x31, other arithmetic, combine_partial(): first_state[2] * first_factor[..., None]  29 us
  transfers between devices with their start and end apart: 5, of which 4 were waited for; matrix products, arithmetic and copies ran while one was open for 9% of the time, Pallas kernels for 0%

commit v1 on v0

--- a/solution.py
+++ b/solution.py
@@ -18,19 +18,9 @@
 MASKED = -1e30
 
 
-def merged(x, axis, combine):
-    everything = jax.tree.map(
-        lambda part, kind: lax.all_gather(part.astype(kind), axis),
-        x,
-        jax.tree.map(lambda a: jnp.bfloat16 if a.dtype == jnp.float32 else a.dtype, x),
-    )
-
-    def take(k):
-        return jax.tree.map(lambda part, own: part[k].astype(own.dtype), everything, x)
-
-    return lax.fori_loop(
-        1, lax.axis_size(axis), lambda k, so_far: combine(so_far, take(k)), take(0)
-    )
+def gather_weight(block):
+    rows = lax.all_gather(block.astype(jnp.bfloat16), "dp", axis=0, tiled=True)
+    return lax.all_gather(rows, "mp", axis=1, tiled=True)
 
 
 def rms_scale(values, scales):
@@ -107,7 +97,7 @@
     return lax.map(one_block, (query_blocks, id_blocks)).reshape(row_count, H, LAT)
 
 
-def page_attention(queries, latent_cache, page_table, cached_lengths, mp_index, score_scale):
+def page_attention(queries, own_score, latent_cache, page_table, cached_lengths, mp_index, score_scale):
     slot_count = latent_cache.shape[0]
     page_rows = latent_cache.shape[1]
     flat_cache = latent_cache.reshape(slot_count * page_rows, latent_cache.shape[2])
@@ -126,7 +116,8 @@
         * score_scale
     )
     scores = jnp.where(allowed[:, None, :], scores, MASKED)
-    peak_score = jnp.max(scores, axis=-1)
+    local_peak = jnp.max(scores, axis=-1)
+    peak_score = jnp.maximum(lax.pmax(local_peak, "mp"), own_score)
     weights = jnp.where(allowed[:, None, :], jnp.exp(scores - peak_score[..., None]), 0.0)
     weight_sum = jnp.sum(weights, axis=-1)
     summed = jnp.einsum(
@@ -135,15 +126,7 @@
         flat_cache[:, :LAT],
         preferred_element_type=jnp.float32,
     )
-    return (peak_score, weight_sum, summed)
-
-
-def combine_partial(first_state, second_state):
-    peak_score = jnp.maximum(first_state[0], second_state[0])
-    first_factor = jnp.exp(first_state[0] - peak_score)
-    second_factor = jnp.exp(second_state[0] - peak_score)
-    weight_sum = first_state[1] * first_factor + second_state[1] * second_factor
-    summed = first_state[2] * first_factor[..., None] + second_state[2] * second_factor[..., None]
+    weight_sum, summed = lax.psum((weight_sum, summed), "mp")
     return (peak_score, weight_sum, summed)
 
 
@@ -163,29 +146,19 @@
     mp_index = lax.axis_index("mp")
     mp_size = lax.axis_size("mp")
     score_scale = (DN + DR) ** (-0.5)
-    trainer = (
-        joined_qkva.astype(jnp.bfloat16),
-        kv_up.astype(jnp.bfloat16),
-        out_proj.astype(jnp.bfloat16),
-    )
     step_full = lax.all_gather(step_rows, "mp", axis=1, tiled=True)
     stacked = jnp.concatenate([prompt_rows, step_full], axis=0)
     normed = rms_scale(stacked, attn_gain).astype(jnp.bfloat16)
     prompt_ids = jnp.arange(prompt_count, dtype=jnp.int32)
     positions = jnp.concatenate([prompt_ids % LEN, cached_lengths], axis=0)
-    served = (
-        lax.all_to_all(trainer[0], "mp", split_axis=0, concat_axis=1, tiled=True),
-        lax.all_to_all(trainer[1], "mp", split_axis=0, concat_axis=1, tiled=True),
-        lax.all_to_all(trainer[2], "mp", split_axis=0, concat_axis=1, tiled=True),
-    )
+    served = tuple(gather_weight(w) for w in (joined_qkva, kv_up, out_proj))
     inputs = normed
     projected = jnp.dot(
         inputs,
-        lax.all_gather(served[0], ("dp", "mp"), axis=0, tiled=True),
+        served[0],
         preferred_element_type=jnp.float32,
     )
-    up_full = lax.all_gather(served[1], ("dp", "mp"), axis=0, tiled=True)
-    up_heads = up_full.reshape(LAT, H, DN + DV)
+    up_heads = served[1].reshape(LAT, H, DN + DV)
     queries, key_rows = queries_keys(
         projected.astype(jnp.bfloat16), positions, latent_gain, up_heads
     )
@@ -196,21 +169,18 @@
     prompt_latent = prompt_attention(
         prompt_queries, prompt_ids, prompt_key_rows, prompt_ids, score_scale
     )
-    partial_state = page_attention(
-        step_queries, latent_cache, page_table, cached_lengths, mp_index, score_scale
-    )
-    peak_score, weight_sum, summed = merged(partial_state, "mp", combine_partial)
     own_score = (
         jnp.einsum("rhc,rc->rh", step_queries, step_keys, preferred_element_type=jnp.float32)
         * score_scale
     )
-    new_peak = jnp.maximum(peak_score, own_score)
-    old_factor = jnp.exp(peak_score - new_peak)
-    own_weight = jnp.exp(own_score - new_peak)
-    weight_sum = weight_sum * old_factor + own_weight
+    peak_score, weight_sum, summed = page_attention(
+        step_queries, own_score, latent_cache, page_table, cached_lengths, mp_index, score_scale
+    )
+    own_weight = jnp.exp(own_score - peak_score)
+    weight_sum = weight_sum + own_weight
     own_latent = step_keys[:, :LAT].astype(jnp.float32)
     own_half = own_weight.astype(jnp.bfloat16).astype(jnp.float32)
-    summed = summed * old_factor[..., None] + own_half[..., None] * own_latent[:, None, :]
+    summed = summed + own_half[..., None] * own_latent[:, None, :]
     step_latent = (summed / weight_sum[..., None]).astype(jnp.bfloat16)
     latent_out = jnp.concatenate([prompt_latent, step_latent], axis=0)
     heads_out = jnp.einsum(
@@ -220,7 +190,7 @@
     inputs = heads_out
     attended = jnp.dot(
         inputs,
-        lax.all_gather(served[2], ("dp", "mp"), axis=0, tiled=True),
+        served[2],
         preferred_element_type=jnp.float32,
     )
     attended = attended.astype(jnp.bfloat16)

time: 1180 us -> 916 us (0.78)
  waiting for transfers between devices: 737 us -> 509 us
  other arithmetic: 70.6 us -> 40.4 us
    all_gather x4 -> x3, waiting for transfers between devices: 728 us -> 366 us  [gather_weight(): return lax.all_gather(rows, 'mp', axis=1, tiled=True)]
    psum x0 -> x1, waiting for transfers between devices: none -> 143 us  [page_attention(): weight_sum, summed = lax.psum((weight_sum, summed), 'mp')]
    all_gather x2 -> x3, blocking collectives: 153 us -> 24.4 us  [gather_weight(): rows = lax.all_gather(block.astype(jnp.bfloat16), 'dp', axis=0, tiled=True)]
    pmax x0 -> x1, blocking collectives: none -> 82 us  [page_attention(): peak_score = jnp.maximum(lax.pmax(local_peak, 'mp'), own_score)]
    psum x0 -> x1, blocking collectives: none -> 76.9 us  [page_attention(): weight_sum, summed = lax.psum((weight_sum, summed), 'mp')]
    add x62 -> x0, other arithmetic: 29.8 us -> none  [the longest x31 29 us: combine_partial(): first_state[2] * first_factor[..., None]]
    all_to_all x2 -> x0, blocking collectives: 29.6 us -> none  [the longest x1 17.6 us: on_device(): lax.all_to_all(trainer[1], 'mp', split_axis=0, concat_axis=1, tiled=True)]
  transfers between devices with their start and end apart: 5 -> 4, of which waited for: 4 -> 4; matrix products, arithmetic and copies ran while one was open for 9% -> 11% of each run, Pallas kernels for 0% -> 0%
where the time goes in v1:
time: 916 us; the launch traced here: 915 us
  waiting for transfers between devices  509 us (56%)
  blocking collectives  266 us (29%)
  matrix products  55.7 us (6%)
  other arithmetic  40.4 us (4%)
  local copies, waits for them, and re-layouts  30.1 us (3%)
  between operations  14 us (2%)
    all_gather x3, waiting for transfers between devices, gather_weight(): return lax.all_gather(rows, 'mp', axis=1, tiled=True)  366 us
    psum x1, waiting for transfers between devices, page_attention(): weight_sum, summed = lax.psum((weight_sum, summed), 'mp')  143 us
    all_gather x1, blocking collectives, on_device(): step_full = lax.all_gather(step_rows, 'mp', axis=1, tiled=True)  82.6 us
    pmax x1, blocking collectives, page_attention(): peak_score = jnp.maximum(lax.pmax(local_peak, 'mp'), own_score)  82 us
    psum x1, blocking collectives, page_attention(): weight_sum, summed = lax.psum((weight_sum, summed), 'mp')  76.9 us
    all_gather x3, blocking collectives, gather_weight(): rows = lax.all_gather(block.astype(jnp.bfloat16), 'dp', axis=0, tiled=True)  24.4 us
    unnamed x26, local copies, waits for them, and re-layouts  21.7 us
  transfers between devices with their start and end apart: 4, of which 4 were waited for; matrix products, arithmetic and copies ran while one was open for 11% of the time, Pallas kernels for 0%

profile of v1, /device:TPU:0, one launch (start us, length us, event | category | flops | bytes accessed | tf_op | source)
XLA Modules:
  0.0 915.3 jit_solution(9291361192338722557)
XLA Ops:
  7.2 1.0 convert_element_type.80
  8.2 9.1 all_gather.22
  17.3 1.0 copy.78
  18.3 7.4 all_gather.24
  25.8 82.6 %all-gather = bf16[32,64,4]{1,2,0:T(4,128)(2,1)S(1)} all-gather(bf16[1,64,4]{1,2,0:T(4,128)(2,1)} %bitcast.53), channel_id=1, replica_groups=mesh['dp'=4,'mp'=32] {'mp'}, dimensions={0}, use_global_device_ids=true | all-gather | bytes 16896 | tf_op jit(solution)/shard_map/all_gather | solution.py:149
  108.5 0.9 compare_reduce_fusion
  109.6 0.9 fusion.44
  110.9 0.7 add_convert_fusion.2
  111.6 2.1 fusion.15
  113.7 0.7 fusion.52
  114.4 92.3 %all-gather.10.cloned.1.call-done = bf16[32,114,2048]{2,1,0:T(8,128)(2,1)} async-done(((bf16[1,114,2048]{2,1,0:T(8,128)(2,1)}), bf16[32,114,2048]{2,1,0:T(8,128)(2,1)}) %all-gather.10.cloned.1.call-update) | async-done | bytes 14942224 | tf_op jit(solution)/shard_map/all_gather | solution.py:23
  206.8 14.3 %reshape.268 = bf16[3648,2048]{1,0:T(8,128)(2,1)} reshape(bf16[32,114,2048]{2,1,0:T(8,128)(2,1)} %all-gather.10.cloned.1.call-done) | data formatting | bytes 29884416
  221.1 15.1 %convolution_convert_fusion = bf16[516,3648]{0,1:T(8,128)(2,1)S(1)} fusion(bf16[3648,2048]{1,0:T(8,128)(2,1)} %reshape.268, f32[2048]{0:T(1024)S(1)} %copy-done.7, f32[516]{0:T(1024)S(1)} %add_rsqrt_fusion.1, bf16[4,2048]{1,0:T(4,128)(2,1)S(1)} %bitcast.48, bf16[512,2048]{1,0:T(8,128)(2,1)S(1)} %copy-done.3), kind=kOutput, calls=%fused_computation.18 | convolution fusion | flops 7719458816 | bytes 20830736 | tf_op jit(solution)/shard_map/dot_general | solution.py:156
  236.2 2.5 slice.84
  238.6 0.9 copy-done.2
  239.5 1.4 slice.87
  240.9 2.0 copy.107
  242.9 2.2 convert_element_type.85
  245.2 0.9 slice_convert_fusion.1
  246.1 0.4 subtract_convert_fusion.1
  246.8 1.3 fusion.28
  248.0 116.4 %all-gather.6.cloned.1.call-done = bf16[512,4096]{0,1:T(8,128)(2,1)} async-done(((bf16[512,128]{0,1:T(8,128)(2,1)}), bf16[512,4096]{0,1:T(8,128)(2,1)}) %all-gather.6.cloned.1.call-update) | async-done | bytes 4194320 | tf_op jit(solution)/shard_map/all_gather | solution.py:23
  364.4 4.9 convert_bitcast_fusion
  369.4 1.4 subtract_convert_fusion
  370.8 1.9 copy-done
  372.8 0.6 copy-done.1
  373.5 0.2 fusion.59
  373.7 82.0 %pmax.7 = f32[4,16]{1,0:T(4,128)S(1)} all-reduce(f32[4,16]{1,0:T(4,128)S(1)} %get-tuple-element.31), channel_id=1, replica_groups=mesh['dp'=4,'mp'=32] {'mp'}, use_global_device_ids=true, to_apply=%region_7.8 | all-reduce | flops 64 | bytes 512 | tf_op jit(solution)/shard_map/pmax | solution.py:120
  455.7 1.3 fusion.30
  457.4 0.2 fusion.37
  457.6 0.7 copy.89
  458.5 7.9 all_gather.26
  466.4 0.2 fusion.32
  466.8 76.9 %psum.15 = f32[4,16]{1,0:T(4,128)S(1)} all-reduce(f32[4,16]{1,0:T(4,128)S(1)} %fusion.38), channel_id=1, replica_groups=mesh['dp'=4,'mp'=32] {'mp'}, use_global_device_ids=true, to_apply=%region_10.11 | all-reduce | flops 64 | bytes 512 | tf_op jit(solution)/shard_map/psum | solution.py:129
  544.1 7.6 pad_maximum_fusion
  551.7 10.6 %fusion.2 = f32[512,16,512]{0,2,1:T(8,128)} fusion(bf16[516,16,576]{2,0,1:T(8,128)(2,1)S(1)} %pad_maximum_fusion, bf16[516,576]{0,1:T(8,128)(2,1)S(1)} %pad_maximum_fusion.3), kind=kOutput, calls=%fused_computation.6 | convolution fusion | flops 4831838208 | bytes 27852800 | tf_op jit(solution)/shard_map/while/body/eval_jaxpr/qhc,kc->qhk/dot_general | solution.py:80
  562.4 17.4 %fusion.60 = (f32[512,16]{0,1:T(8,128)S(1)}, bf16[512,16,512]{0,2,1:T(8,128)(2,1)}) fusion(f32[512,16,512]{0,2,1:T(8,128)} %fusion.2, pred[512,512]{0,1:T(8,128)(4,1)S(1)} %fusion.32), kind=kOutput, calls=%fused_computation.100 | output fusion | flops 33554944 | bytes 25460736 | tf_op jit(solution)/shard_map/while/body/eval_jaxpr/sub | solution.py:87
  579.7 10.1 %divide_convert_fusion = bf16[512,16,512]{2,0,1:T(8,128)(2,1)} fusion(f32[512,16]{0,1:T(8,128)S(1)} %get-tuple-element.33, bf16[512,16,512]{0,2,1:T(8,128)(2,1)} %get-tuple-element.34, bf16[516,512]{0,1:T(8,128)(2,1)S(1)} %fusion.30), kind=kOutput, calls=%fused_computation.1 | convolution fusion | flops 4303355904 | bytes 17334272 | tf_op jit(solution)/shard_map/while/body/eval_jaxpr/qhk,kl->qhl/dot_general | solution.py:89
  589.8 142.6 %all-reduce.2.cloned.1.call-done = f32[4,16,512]{2,0,1:T(4,128)} async-done(((f32[4,16,512]{2,0,1:T(4,128)}), f32[4,16,512]{2,0,1:T(4,128)}) %all-reduce.2.cloned.1.call-update) | async-done | bytes 131088 | tf_op jit(solution)/shard_map/psum | solution.py:129
  732.5 1.0 fusion.33
  733.5 6.4 convert_bitcast_fusion.1
  739.9 0.3 copy.94
  740.2 0.4 pad.18
  740.5 0.6 copy.109
  741.1 157.6 %all-gather.8.cloned.1.call-done = bf16[2048,2048]{0,1:T(8,128)(2,1)} async-done(((bf16[2048,64]{0,1:T(8,128)(2,1)}), bf16[2048,2048]{0,1:T(8,128)(2,1)}) %all-gather.8.cloned.1.call-update) | async-done | bytes 8388624 | tf_op jit(solution)/shard_map/all_gather | solution.py:23
  898.7 8.0 convolution_convert_fusion.1
  906.7 1.5 slice.100
  908.2 0.6 constant_dynamic-slice_fusion
  (59 shorter events, 2.5 us)
Async XLA Ops:
  7.2 199.6 %all-gather.10.cloned.1.call-start = ((), (), s32[]{:S(2)}) async-start(), calls=%async_computation.3 | async-start | bytes 16220160 | tf_op jit(solution)/shard_map/all_gather | solution.py:23
  17.3 347.1 %all-gather.6.cloned.1.call-start = ((), (), s32[]{:S(2)}) async-start(), calls=%async_computation | async-start | bytes 4325376 | tf_op jit(solution)/shard_map/all_gather | solution.py:23
  25.7 706.8 %all-reduce.2.cloned.1.call-start = ((), (), s32[]{:S(2)}) async-start(), calls=%async_computation.1 | async-start | bytes 262144 | tf_op jit(solution)/shard_map/psum | solution.py:129
  114.4 106.6 %copy-start.3 = (bf16[512,2048]{1,0:T(8,128)(2,1)S(1)}, bf16[512,2048]{1,0:T(8,128)(2,1)}, u32[]{:S(2)}) copy-start(bf16[512,2048]{1,0:T(8,128)(2,1)} %param.10) | copy-start | bytes 6291460
  114.4 106.6 %copy-start.7 = (f32[2048]{0:T(1024)S(1)}, f32[2048]{0:T(1024)}, u32[]{:S(2)}) copy-start(f32[2048]{0:T(1024)} %param.12) | copy-start | bytes 24580
  236.1 3.3 copy-start.2
  364.4 5.0 slice-start
  364.4 5.0 slice-start.1
  369.4 3.3 copy-start
  370.8 2.5 copy-start.1
  372.7 0.8 copy-start.5
  372.7 83.0 %copy-start.6 = (f32[512]{0:T(512)S(1)}, f32[512]{0:T(512)}, u32[]{:S(2)}) copy-start(f32[512]{0:T(512)} %param.13) | copy-start | bytes 6148
  372.7 85.8 %copy-start.4 = (f32[512,64]{0,1:T(8,128)S(1)}, f32[512,64]{0,1:T(8,128)}, u32[]{:S(2)}) copy-start(f32[512,64]{0,1:T(8,128)} %param.16) | copy-start | bytes 393220
  458.4 440.3 %all-gather.8.cloned.1.call-start = ((), (), s32[]{:S(2)}) async-start(), calls=%async_computation.2 | async-start | bytes 8650752 | tf_op jit(solution)/shard_map/all_gather | solution.py:23
Sparse Core Ops, SparseCore 0:
  17.4 189.3 all-gather.9
  208.4 155.9 all-gather.5
  458.5 273.9 all-reduce.1
  734.1 164.5 all-gather.7

commit v2 on v1

--- a/solution.py
+++ b/solution.py
@@ -1,4 +1,6 @@
 import math
+
+import numpy as np
 
 import jax
 import jax.numpy as jnp
@@ -18,9 +20,84 @@
 MASKED = -1e30
 
 
-def gather_weight(block):
-    rows = lax.all_gather(block.astype(jnp.bfloat16), "dp", axis=0, tiled=True)
-    return lax.all_gather(rows, "mp", axis=1, tiled=True)
+AXES = ("dp", "mp")
+
+
+def _coords(i):
+    dp, mp = i // 32, i % 32
+    return (2 * (dp // 2) + (mp // 4) % 2, mp % 4, mp // 8, dp % 2)
+
+
+def _index(x, y, z, core):
+    return ((x // 2) * 2 + core) * 32 + z * 8 + (x % 2) * 4 + y
+
+
+def _shift_pairs(dim, step):
+    pairs = []
+    for i in range(128):
+        c = list(_coords(i))
+        c[dim] = (c[dim] + step) % 4
+        pairs.append((i, _index(*c)))
+    return pairs
+
+
+def torus_gather(block, cuts):
+    rows = block.shape[0]
+    partner = lax.ppermute(block, "dp", [(d, d ^ 1) for d in range(4)])
+    chip = jnp.concatenate([block, partner], axis=0)
+    me = lax.axis_index(AXES)
+    dp, mp = me // 32, me % 32
+    cx, cy, cz, ccore = 2 * (dp // 2) + (mp // 4) % 2, mp % 4, mp // 8, dp % 2
+    ids = np.arange(128)
+    x = 2 * (ids // 64) + (ids % 32 // 4) % 2
+    y = ids % 4
+    z = ids % 32 // 8
+    core = (ids // 32) % 2
+    rel = ((x - cx) % 4) * 16 + ((y - cy) % 4) * 4 + (z - cz) % 4
+    pieces = []
+    for part in range(len(cuts) - 1):
+        data = chip[:, cuts[part]:cuts[part + 1]]
+        offs = [(0, 0, 0)]
+        for stage in range(3):
+            dim = (part + stage) % 3
+            right = lax.ppermute(data, AXES, _shift_pairs(dim, 1))
+            left = lax.ppermute(data, AXES, _shift_pairs(dim, -1))
+            far = lax.ppermute(right, AXES, _shift_pairs(dim, 1))
+            new_offs = list(offs)
+            for delta in (-1, 1, -2):
+                for o in offs:
+                    o = list(o)
+                    o[dim] = (o[dim] + delta) % 4
+                    new_offs.append(tuple(o))
+            data = jnp.concatenate([data, right, left, far], axis=0)
+            offs = new_offs
+        table = np.zeros((4, 4, 4), np.int32)
+        for pos, o in enumerate(offs):
+            table[o] = pos
+        pick = jnp.take(jnp.asarray(table.reshape(-1)), rel, mode="clip") * 2 + (core - ccore) % 2
+        slabs = data.reshape(-1, rows, data.shape[-1])
+        pieces.append(jnp.take(slabs, pick, axis=0, mode="clip"))
+    return jnp.concatenate(pieces, axis=2)
+
+
+def gather_weights(joined, kv_up, out_proj):
+    mp_size = 32
+    j = joined.astype(jnp.bfloat16).reshape(mp_size, -1)
+    k = kv_up.astype(jnp.bfloat16).reshape(mp_size, -1)
+    o = out_proj.astype(jnp.bfloat16).reshape(mp_size, -1)
+    packed = jnp.concatenate([j, k, o], axis=1)
+    swapped = lax.all_to_all(packed, "mp", 0, 0, tiled=True)
+    jw, kw = j.shape[1], k.shape[1]
+    jr = swapped[:, :jw].reshape(mp_size, 16, 114).transpose(1, 0, 2).reshape(16, mp_size * 114)
+    kr = swapped[:, jw:jw + kw].reshape(mp_size, 4, 128).transpose(1, 0, 2).reshape(16, 1024)
+    orr = swapped[:, jw + kw:].reshape(mp_size, 16, 64).transpose(1, 0, 2).reshape(16, mp_size * 64)
+    jr = jnp.pad(jr, ((0, 0), (0, 3712 - 3648)))
+    block = jnp.concatenate([jr, orr, kr], axis=1)
+    g = torus_gather(block, [0, 2304, 4608, 6784])
+    w1 = g[:, :, :3648].reshape(2048, 3648)
+    w3 = g[:, :, 3712:5760].reshape(2048, 2048)
+    w2 = g[:, :, 5760:].reshape(128, 4, 4096).reshape(512, 4096)
+    return w1, w2, w3
 
 
 def rms_scale(values, scales):
@@ -97,37 +174,31 @@
     return lax.map(one_block, (query_blocks, id_blocks)).reshape(row_count, H, LAT)
 
 
-def page_attention(queries, own_score, latent_cache, page_table, cached_lengths, mp_index, score_scale):
-    slot_count = latent_cache.shape[0]
-    page_rows = latent_cache.shape[1]
-    flat_cache = latent_cache.reshape(slot_count * page_rows, latent_cache.shape[2])
-    slot_ids = mp_index * slot_count + jnp.arange(slot_count, dtype=jnp.int32)
-    matches = page_table[:, :, None] == slot_ids[None, None, :]
-    owned = jnp.any(matches, axis=1)
-    page_numbers = jnp.arange(page_table.shape[1], dtype=jnp.int32)[None, :, None]
-    page_index = jnp.sum(jnp.where(matches, page_numbers, 0), axis=1)
-    key_position = (
-        page_index[:, :, None] * page_rows + jnp.arange(page_rows, dtype=jnp.int32)[None, None, :]
-    )
-    allowed = owned[:, :, None] & (key_position < cached_lengths[:, None, None])
-    allowed = allowed.reshape(page_table.shape[0], slot_count * page_rows)
+def step_attention(queries, own_keys, latent_cache, page_table, cached_lengths, score_scale):
+    pool = lax.all_gather(latent_cache, "mp", axis=0, tiled=True)
+    request_count, page_count = page_table.shape
+    page_rows = pool.shape[1]
+    pages = pool[page_table].reshape(request_count, page_count * page_rows, pool.shape[2])
+    key_all = jnp.concatenate([pages, own_keys[:, None, :]], axis=1)
+    cached_ok = (
+        jnp.arange(page_count * page_rows, dtype=jnp.int32)[None, :] < cached_lengths[:, None]
+    )
+    allowed = jnp.concatenate([cached_ok, jnp.ones((request_count, 1), jnp.bool_)], axis=1)
     scores = (
-        jnp.einsum("rhc,kc->rhk", queries, flat_cache, preferred_element_type=jnp.float32)
+        jnp.einsum("rhc,rkc->rhk", queries, key_all, preferred_element_type=jnp.float32)
         * score_scale
     )
     scores = jnp.where(allowed[:, None, :], scores, MASKED)
-    local_peak = jnp.max(scores, axis=-1)
-    peak_score = jnp.maximum(lax.pmax(local_peak, "mp"), own_score)
-    weights = jnp.where(allowed[:, None, :], jnp.exp(scores - peak_score[..., None]), 0.0)
-    weight_sum = jnp.sum(weights, axis=-1)
+    peak_score = jnp.max(scores, axis=-1, keepdims=True)
+    weights = jnp.where(allowed[:, None, :], jnp.exp(scores - peak_score), 0.0)
+    weight_sum = jnp.sum(weights, axis=-1, keepdims=True)
     summed = jnp.einsum(
-        "rhk,kl->rhl",
+        "rhk,rkl->rhl",
         weights.astype(jnp.bfloat16),
-        flat_cache[:, :LAT],
+        key_all[:, :, :LAT],
         preferred_element_type=jnp.float32,
     )
-    weight_sum, summed = lax.psum((weight_sum, summed), "mp")
-    return (peak_score, weight_sum, summed)
+    return (summed / weight_sum).astype(jnp.bfloat16)
 
 
 def on_device(
@@ -151,7 +222,7 @@
     normed = rms_scale(stacked, attn_gain).astype(jnp.bfloat16)
     prompt_ids = jnp.arange(prompt_count, dtype=jnp.int32)
     positions = jnp.concatenate([prompt_ids % LEN, cached_lengths], axis=0)
-    served = tuple(gather_weight(w) for w in (joined_qkva, kv_up, out_proj))
+    served = gather_weights(joined_qkva, kv_up, out_proj)
     inputs = normed
     projected = jnp.dot(
         inputs,
@@ -169,19 +240,9 @@
     prompt_latent = prompt_attention(
         prompt_queries, prompt_ids, prompt_key_rows, prompt_ids, score_scale
     )
-    own_score = (
-        jnp.einsum("rhc,rc->rh", step_queries, step_keys, preferred_element_type=jnp.float32)
-        * score_scale
-    )
-    peak_score, weight_sum, summed = page_attention(
-        step_queries, own_score, latent_cache, page_table, cached_lengths, mp_index, score_scale
-    )
-    own_weight = jnp.exp(own_score - peak_score)
-    weight_sum = weight_sum + own_weight
-    own_latent = step_keys[:, :LAT].astype(jnp.float32)
-    own_half = own_weight.astype(jnp.bfloat16).astype(jnp.float32)
-    summed = summed + own_half[..., None] * own_latent[:, None, :]
-    step_latent = (summed / weight_sum[..., None]).astype(jnp.bfloat16)
+    step_latent = step_attention(
+        step_queries, step_keys, latent_cache, page_table, cached_lengths, score_scale
+    )
     latent_out = jnp.concatenate([prompt_latent, step_latent], axis=0)
     heads_out = jnp.einsum(
         "rhl,lhv->rhv", latent_out, up_heads[..., DN:], preferred_element_type=jnp.float32

time: 916 us -> 477 us (0.52)
  waiting for transfers between devices: 509 us -> 45.8 us
  blocking collectives: 266 us -> 120 us
  local copies, waits for them, and re-layouts: 30.1 us -> 119 us
  starting transfers between devices: 0.16 us -> 37.5 us
  other arithmetic: 40.4 us -> 65.4 us
    all_gather x3 -> x1, waiting for transfers between devices: 366 us -> 0.02 us  [step_attention(): pool = lax.all_gather(latent_cache, 'mp', axis=0, tiled=True)]
    psum x1 -> x0, waiting for transfers between devices: 143 us -> none  [page_attention(): weight_sum, summed = lax.psum((weight_sum, summed), 'mp')]
    pmax x1 -> x0, blocking collectives: 82 us -> none  [page_attention(): peak_score = jnp.maximum(lax.pmax(local_peak, 'mp'), own_score)]
    psum x1 -> x0, blocking collectives: 76.9 us -> none  [page_attention(): weight_sum, summed = lax.psum((weight_sum, summed), 'mp')]
    ppermute x0 -> x28, waiting for transfers between devices: none -> 41.8 us  [the longest x9 20.2 us: torus_gather(): left = lax.ppermute(data, AXES, _shift_pairs(dim, -1))]
    gather x0 -> x7, local copies, waits for them, and re-layouts: none -> 39.1 us  [the longest x3 32.3 us: torus_gather(): pieces.append(jnp.take(slabs, pick, axis=0, mode='clip'))]
    all_gather x1, blocking collectives: 82.6 us -> 120 us  [on_device(): step_full = lax.all_gather(step_rows, 'mp', axis=1, tiled=True)]
    ppermute x0 -> x28, starting transfers between devices: none -> 28.1 us  [the longest x9 17.9 us: torus_gather(): left = lax.ppermute(data, AXES, _shift_pairs(dim, -1))]
  transfers between devices with their start and end apart: 4 -> 30, of which waited for: 4 -> 10; matrix products, arithmetic and copies ran while one was open for 11% -> 20% of each run, Pallas kernels for 0% -> 0%
where the time goes in v2:
time: 477 us; the launch traced here: 468 us
  blocking collectives  120 us (25%)
  local copies, waits for them, and re-layouts  119 us (25%)
  other arithmetic  65.4 us (14%)
  matrix products  64 us (13%)
  waiting for transfers between devices  45.8 us (10%)
  starting transfers between devices  37.5 us (8%)
  between operations  15.2 us (3%)
    all_gather x1, blocking collectives, on_device(): step_full = lax.all_gather(step_rows, 'mp', axis=1, tiled=True)  120 us
    unnamed x68, local copies, waits for them, and re-layouts  41.1 us
    gather x3, local copies, waits for them, and re-layouts, torus_gather(): pieces.append(jnp.take(slabs, pick, axis=0, mode='clip'))  32.3 us
    dot_general x1, matrix products, on_device(): projected = jnp.dot(inputs, served[0], preferred_element_type=jnp.float32)  24.8 us
    concatenate x2, other arithmetic, torus_gather(): return jnp.concatenate(pieces, axis=2)  21.2 us
    ppermute x9, waiting for transfers between devices, torus_gather(): left = lax.ppermute(data, AXES, _shift_pairs(dim, -1))  20.2 us
    sub x1, other arithmetic, one_block(): weights = jnp.where(allowed[:, None, :], jnp.exp(scores - peak_score), 0.0)  18.2 us
    ppermute x9, starting transfers between devices, torus_gather(): left = lax.ppermute(data, AXES, _shift_pairs(dim, -1))  17.9 us
  transfers between devices with their start and end apart: 30, of which 10 were waited for; matrix products, arithmetic and copies ran while one was open for 20% of the time, Pallas kernels for 0%

profile of v2, /device:TPU:0, one launch (start us, length us, event | category | flops | bytes accessed | tf_op | source)
XLA Modules:
  0.0 467.6 jit_solution(11798314766939178893)
XLA Ops:
  12.9 9.3 %all-to-all-start = ((bf16[32,2,1680]{2,1,0:T(2,128)(2,1)}), bf16[32,2,1680]{2,1,0:T(2,128)(2,1)S(1)}, u32[]{:S(2)}, u32[]{:S(2)}) async-start(bf16[32,2,1680]{2,1,0:T(2,128)(2,1)} %reshape.350), calls=%async_computation | async-start | bytes 458752 | tf_op jit(solution)/shard_map/all_to_all | solution.py:89
  28.0 3.3 all-to-all-done
  36.0 2.4 collective-permute-start.20
  39.9 2.5 collective-permute-start.11
  44.4 5.0 %collective-permute-done.1 = bf16[32,2176]{1,0:T(8,128)(2,1)S(1)} collective-permute-done((bf16[32,2176]{1,0:T(8,128)(2,1)S(1)}, bf16[32,2176]{1,0:T(8,128)(2,1)S(1)}, u32[]{:S(2)}, u32[]{:S(2)}) %collective-permute-start.1) | collective-permute-done | bytes 139296 | tf_op jit(solution)/shard_map/ppermute | solution.py:63
  50.2 4.2 collective-permute-done.2
  58.2 2.5 collective-permute-done.3
  60.8 3.2 collective-permute-start.5
  64.9 3.2 collective-permute-start.23
  69.7 3.8 collective-permute-done.4
  73.5 2.2 collective-permute-start.14
  79.8 3.0 collective-permute-done.13
  86.3 3.5 collective-permute-done.6
  92.1 3.2 collective-permute-start.8
  98.0 2.3 collective-permute-done.15
  104.2 120.2 %all-gather = bf16[32,64,4]{1,2,0:T(4,128)(2,1)S(1)} all-gather(bf16[1,64,4]{1,2,0:T(4,128)(2,1)S(1)} %bitcast.71), channel_id=1, replica_groups=mesh['dp'=4,'mp'=32] {'mp'}, dimensions={0}, use_global_device_ids=true | all-gather | bytes 16896 | tf_op jit(solution)/shard_map/all_gather | solution.py:220
  224.5 2.1 fusion.16
  227.0 2.8 gather_fusion.6
  230.1 3.2 constant_dynamic-update-slice_fusion.9
  233.3 3.2 constant_dynamic-update-slice_fusion.8
  236.5 2.1 collective-permute-start.18
  240.1 3.3 constant_dynamic-update-slice_fusion.26
  243.4 3.2 constant_dynamic-update-slice_fusion.42
  246.6 16.0 %collective-permute-done.17 = bf16[512,2304]{1,0:T(8,128)(2,1)} collective-permute-done((bf16[512,2304]{1,0:T(8,128)(2,1)}, bf16[512,2304]{1,0:T(8,128)(2,1)}, u32[]{:S(2)}, u32[]{:S(2)}) %collective-permute-start.17) | collective-permute-done | bytes 2359328 | tf_op jit(solution)/shard_map/ppermute | solution.py:64
  262.6 3.2 constant_dynamic-update-slice_fusion.25
  267.4 10.5 %gather_fusion.1 = bf16[128,16,2176]{2,1,0:T(8,128)(2,1)} fusion(bf16[128,16,2176]{2,1,0:T(8,128)(2,1)} %bitcast.4, s32[1024]{0:T(1024)S(1)} %pad_clamp_fusion.3), kind=kCustom, calls=%fused_computation.1 | custom fusion | bytes 17826304 | tf_op jit(solution)/shard_map/jit(_take)/gather | solution.py:79
  277.9 5.1 %slice.133 = bf16[128,16,1024]{2,1,0:T(8,128)(2,1)} slice(bf16[128,16,2176]{2,1,0:T(8,128)(2,1)} %gather_fusion.1), slice={[0:128], [0:16], [1152:2176]} | slice | bytes 8388608 | tf_op jit(solution)/shard_map/slice | solution.py:99
  283.0 7.5 %reshape_reshape_reshape.3 = bf16[512,16,256]{2,1,0:T(8,128)(2,1)} reshape(bf16[128,16,1024]{2,1,0:T(8,128)(2,1)} %slice.133) | data formatting | bytes 8388608 | tf_op jit(solution)/shard_map/reshape;reshape;reshape | solution.py:232
  290.5 5.0 %fusion.70 = (bf16[512,16,128]{2,1,0:T(8,128)(2,1)}, bf16[512,16,128]{2,1,0:T(8,128)(2,1)}) fusion(bf16[512,16,256]{2,1,0:T(8,128)(2,1)} %reshape_reshape_reshape.3), kind=kLoop, calls=%fused_computation.196 | loop fusion | bytes 8388608 | tf_op jit(solution)/shard_map/slice | solution.py:248
  295.5 3.2 constant_dynamic-update-slice_fusion.41
  298.8 10.9 %gather_fusion.5 = bf16[128,16,2304]{2,1,0:T(8,128)(2,1)} fusion(bf16[128,16,2304]{2,1,0:T(8,128)(2,1)} %bitcast.9, s32[1024]{0:T(1024)S(1)} %pad_clamp_fusion.1), kind=kCustom, calls=%fused_computation.5 | custom fusion | bytes 18874880 | tf_op jit(solution)/shard_map/jit(_take)/gather | solution.py:79
  309.7 3.3 constant_dynamic-update-slice_fusion.24
  313.0 10.8 %gather_fusion.3 = bf16[128,16,2304]{2,1,0:T(8,128)(2,1)} fusion(bf16[128,16,2304]{2,1,0:T(8,128)(2,1)} %bitcast.8, s32[1024]{0:T(1024)S(1)} %pad_clamp_fusion.2), kind=kCustom, calls=%fused_computation.3 | custom fusion | bytes 18874880 | tf_op jit(solution)/shard_map/jit(_take)/gather | solution.py:79
  323.8 12.9 %pad_maximum_fusion = bf16[128,16,3648]{2,1,0:T(8,128)(2,1)} fusion(bf16[128,16,2304]{2,1,0:T(8,128)(2,1)} %gather_fusion.5, bf16[128,16,2304]{2,1,0:T(8,128)(2,1)} %gather_fusion.3), kind=kLoop, calls=%fused_computation.12 | loop fusion | flops 29884416 | bytes 33816576 | tf_op jit(solution)/shard_map/concatenate | solution.py:80
  336.7 24.8 %convolution_convert_fusion = bf16[516,3648]{0,1:T(8,128)(2,1)S(1)} fusion(bf16[2048,3648]{1,0:T(8,128)(2,1)} %bitcast.55, f32[2048]{0:T(1024)S(1)} %copy-done.14, f32[516]{0:T(1024)S(1)} %add_rsqrt_fusion.1, bf16[4,2048]{1,0:T(4,128)(2,1)S(1)} %bitcast.70, bf16[512,2048]{1,0:T(8,128)(2,1)S(1)} %copy-done.5), kind=kOutput, calls=%fused_computation.28 | convolution fusion | flops 7719458816 | bytes 20830736 | tf_op jit(solution)/shard_map/dot_general | solution.py:227
  361.7 2.3 slice.136
  364.8 2.5 slice.138
  367.4 3.0 copy.113
  370.4 2.3 convert_element_type.79
  372.9 5.0 %convert_bitcast_fusion = bf16[516,16,512]{2,0,1:T(8,128)(2,1)S(1)} fusion(bf16[516,16,192]{0,2,1:T(8,128)(2,1)} %bitcast.54, bf16[512,16,128]{2,1,0:T(8,128)(2,1)} %get-tuple-element.34), kind=kOutput, calls=%fused_computation.21 | convolution fusion | flops 1086357504 | bytes 13172736 | tf_op jit(solution)/shard_map/rhn,lhn->rhl/dot_general | solution.py:138
  379.4 1.9 copy-done.2
  383.6 12.3 %pad_maximum_fusion.1 = bf16[516,16,576]{2,0,1:T(8,128)(2,1)} fusion(bf16[516,16,32]{2,0,1:T(8,128)(2,1)} %copy-done.4, bf16[516,16,32]{2,0,1:T(8,128)(2,1)} %copy-done.3, bf16[516,16,512]{2,0,1:T(8,128)(2,1)} %copy-done.2), kind=kLoop, calls=%fused_computation.14 | loop fusion | flops 28532736 | bytes 19021824 | tf_op jit(solution)/shard_map/concatenate | solution.py:141
  396.0 8.3 %pad_maximum_fusion.2 = bf16[128,16,2048]{2,1,0:T(8,128)(2,1)} fusion(bf16[128,16,2176]{2,1,0:T(8,128)(2,1)} %gather_fusion.1, bf16[128,16,2304]{2,1,0:T(8,128)(2,1)} %gather_fusion.5), kind=kLoop, calls=%fused_computation.22 | loop fusion | flops 16777216 | bytes 26738688 | tf_op jit(solution)/shard_map/concatenate | solution.py:80
  405.2 12.8 %fusion.3 = f32[512,16,512]{0,2,1:T(8,128)} fusion(bf16[516,16,576]{2,0,1:T(8,128)(2,1)} %pad_maximum_fusion.1, bf16[516,576]{0,1:T(8,128)(2,1)S(1)} %pad_maximum_fusion.5), kind=kOutput, calls=%fused_computation.15 | convolution fusion | flops 4831838208 | bytes 27852800 | tf_op jit(solution)/shard_map/while/body/eval_jaxpr/qhc,kc->qhk/dot_general | solution.py:157
  418.0 18.2 %fusion.72 = (f32[512,16]{0,1:T(8,128)}, bf16[512,16,512]{0,2,1:T(8,128)(2,1)}) fusion(f32[512,16,512]{0,2,1:T(8,128)} %fusion.3, pred[512,512]{0,1:T(8,128)(4,1)S(1)} %fusion.36), kind=kOutput, calls=%fused_computation.198 | output fusion | flops 33554944 | bytes 25460736 | tf_op jit(solution)/shard_map/while/body/eval_jaxpr/sub | solution.py:164
  436.1 10.2 %divide_convert_fusion = bf16[512,16,512]{2,0,1:T(8,128)(2,1)} fusion(f32[512,16]{0,1:T(8,128)} %get-tuple-element.81, bf16[512,16,512]{0,2,1:T(8,128)(2,1)} %get-tuple-element.82, bf16[516,512]{0,1:T(8,128)(2,1)S(1)} %fusion.31), kind=kOutput, calls=%fused_computation.9 | convolution fusion | flops 4303355904 | bytes 17334272 | tf_op jit(solution)/shard_map/while/body/eval_jaxpr/qhk,kl->qhl/dot_general | solution.py:166
  446.4 5.8 %convert_bitcast_fusion.1 = bf16[516,16,128]{2,0,1:T(8,128)(2,1)S(1)} fusion(bf16[4,16,512]{2,0,1:T(4,128)(2,1)S(1)} %copy-done.8, bf16[512,16,512]{2,0,1:T(8,128)(2,1)} %divide_convert_fusion, bf16[512,16,128]{2,1,0:T(8,128)(2,1)S(1)} %copy-done.6), kind=kOutput, calls=%fused_computation.39 | convolution fusion | flops 1100095488 | bytes 12664832 | tf_op jit(solution)/shard_map/rhl,lhv->rhv/dot_general | solution.py:247
  453.4 4.9 %convolution_convert_fusion.1 = bf16[516,2048]{1,0:T(8,128)(2,1)S(1)} fusion(bf16[516,2048]{1,0:T(8,128)(2,1)S(1)} %bitcast.60, bf16[2048,2048]{1,0:T(8,128)(2,1)S(1)} %bitcast.59), kind=kOutput, calls=%fused_computation.36 | convolution fusion | flops 4329578496 | bytes 12615680 | tf_op jit(solution)/shard_map/dot_general | solution.py:252
  (182 shorter events, 55.7 us)
Async XLA Ops:
  7.2 18.3 %copy-start.1 = (s32[64]{0:T(128)S(1)}, s32[64]{0:T(128)}, u32[]{:S(2)}) copy-start(s32[64]{0:T(128)} %constant.223.clone) | copy-start | bytes 772
  7.2 19.5 %copy-start = (s32[64]{0:T(128)S(1)}, s32[64]{0:T(128)}, u32[]{:S(2)}) copy-start(s32[64]{0:T(128)} %constant.225.clone) | copy-start | bytes 772
  7.2 20.8 %copy-start.12 = (s32[128]{0:T(128)S(1)}, s32[128]{0:T(128)}, u32[]{:S(2)}) copy-start(s32[128]{0:T(128)} %constant.224.clone) | copy-start | bytes 1540
  7.2 20.7 %copy-start.10 = (s32[4,8]{1,0:T(4,128)S(1)}, s32[4,8]{1,0:T(4,128)}, u32[]{:S(2)}) copy-start(s32[4,8]{1,0:T(4,128)} %param.25) | copy-start | bytes 388
  12.9 18.4 %all-to-all-start = ((bf16[32,2,1680]{2,1,0:T(2,128)(2,1)}), bf16[32,2,1680]{2,1,0:T(2,128)(2,1)S(1)}, u32[]{:S(2)}, u32[]{:S(2)}) async-start(bf16[32,2,1680]{2,1,0:T(2,128)(2,1)} %reshape.350), calls=%async_computation | async-start | bytes 458752 | tf_op jit(solution)/shard_map/all_to_all | solution.py:89
  22.3 204.7 %all-gather.3.cloned.1.call-start = ((), (), s32[]{:S(2)}) async-start(), calls=%async_computation.1 | async-start | bytes 1351680 | tf_op jit(solution)/shard_map/all_gather | solution.py:178
  32.9 1.6 collective-permute-start
  35.2 20.0 %collective-permute-start.19 = (bf16[32,2304]{1,0:T(8,128)(2,1)S(1)}, bf16[32,2304]{1,0:T(8,128)(2,1)S(1)}, u32[]{:S(2)}, u32[]{:S(2)}) collective-permute-start(bf16[32,2304]{1,0:T(8,128)(2,1)S(1)} %get-tuple-element.54), channel_id=1, source_target_pairs={{0,1},{1,2},{2,3},{3,0},{4,5},{5,6},{6,7},{7,4},{8,9},{9,10},{10,1... | collective-permute-start | bytes 442376 | tf_op jit(solution)/shard_map/ppermute | solution.py:63
  36.0 20.7 %collective-permute-start.20 = (bf16[32,2304]{1,0:T(8,128)(2,1)S(1)}, bf16[32,2304]{1,0:T(8,128)(2,1)S(1)}, u32[]{:S(2)}, u32[]{:S(2)}) collective-permute-start(bf16[32,2304]{1,0:T(8,128)(2,1)S(1)} %get-tuple-element.54), channel_id=1, source_target_pairs={{0,3},{1,0},{2,1},{3,2},{4,7},{5,4},{6,5},{7,6},{8,11},{9,8},{10,9... | collective-permute-start | bytes 442376 | tf_op jit(solution)/shard_map/ppermute | solution.py:64
  39.1 16.0 %collective-permute-start.10 = (bf16[32,2304]{1,0:T(8,128)(2,1)S(1)}, bf16[32,2304]{1,0:T(8,128)(2,1)S(1)}, u32[]{:S(2)}, u32[]{:S(2)}) collective-permute-start(bf16[32,2304]{1,0:T(8,128)(2,1)S(1)} %get-tuple-element.28), channel_id=1, source_target_pairs={{0,4},{1,5},{2,6},{3,7},{4,64},{5,65},{6,66},{7,67},{8,12},{9,13},... | collective-permute-start | bytes 442376 | tf_op jit(solution)/shard_map/ppermute | solution.py:63
  39.9 17.6 %collective-permute-start.11 = (bf16[32,2304]{1,0:T(8,128)(2,1)S(1)}, bf16[32,2304]{1,0:T(8,128)(2,1)S(1)}, u32[]{:S(2)}, u32[]{:S(2)}) collective-permute-start(bf16[32,2304]{1,0:T(8,128)(2,1)S(1)} %get-tuple-element.28), channel_id=1, source_target_pairs={{0,68},{1,69},{2,70},{3,71},{4,0},{5,1},{6,2},{7,3},{8,76},{9,77},... | collective-permute-start | bytes 442376 | tf_op jit(solution)/shard_map/ppermute | solution.py:64
  43.1 6.3 %collective-permute-start.1 = (bf16[32,2176]{1,0:T(8,128)(2,1)S(1)}, bf16[32,2176]{1,0:T(8,128)(2,1)S(1)}, u32[]{:S(2)}, u32[]{:S(2)}) collective-permute-start(bf16[32,2176]{1,0:T(8,128)(2,1)S(1)} %get-tuple-element.19), channel_id=1, source_target_pairs={{0,8},{1,9},{2,10},{3,11},{4,12},{5,13},{6,14},{7,15},{8,16},{9,17... | collective-permute-start | bytes 417800 | tf_op jit(solution)/shard_map/ppermute | solution.py:63
  49.3 5.1 %collective-permute-start.2 = (bf16[32,2176]{1,0:T(8,128)(2,1)S(1)}, bf16[32,2176]{1,0:T(8,128)(2,1)S(1)}, u32[]{:S(2)}, u32[]{:S(2)}) collective-permute-start(bf16[32,2176]{1,0:T(8,128)(2,1)S(1)} %get-tuple-element.19), channel_id=1, source_target_pairs={{0,24},{1,25},{2,26},{3,27},{4,28},{5,29},{6,30},{7,31},{8,0},{9,1... | collective-permute-start | bytes 417800 | tf_op jit(solution)/shard_map/ppermute | solution.py:64
  54.4 6.3 %collective-permute-start.3 = (bf16[32,2176]{1,0:T(8,128)(2,1)S(1)}, bf16[32,2176]{1,0:T(8,128)(2,1)S(1)}, u32[]{:S(2)}, u32[]{:S(2)}) collective-permute-start(bf16[32,2176]{1,0:T(8,128)(2,1)S(1)} %collective-permute-done.1), channel_id=1, source_target_pairs={{0,8},{1,9},{2,10},{3,11},{4,12},{5,13},{6,14},{7,15},{8,16},{9,17... | collective-permute-start | bytes 417800 | tf_op jit(solution)/shard_map/ppermute | solution.py:65
  55.1 9.6 %collective-permute-start.21 = (bf16[32,2304]{1,0:T(8,128)(2,1)S(1)}, bf16[32,2304]{1,0:T(8,128)(2,1)S(1)}, u32[]{:S(2)}, u32[]{:S(2)}) collective-permute-start(bf16[32,2304]{1,0:T(8,128)(2,1)S(1)} %collective-permute-done.19), channel_id=1, source_target_pairs={{0,1},{1,2},{2,3},{3,0},{4,5},{5,6},{6,7},{7,4},{8,9},{9,10},{10,1... | collective-permute-start | bytes 442376 | tf_op jit(solution)/shard_map/ppermute | solution.py:65
  55.1 13.0 %collective-permute-start.12 = (bf16[32,2304]{1,0:T(8,128)(2,1)S(1)}, bf16[32,2304]{1,0:T(8,128)(2,1)S(1)}, u32[]{:S(2)}, u32[]{:S(2)}) collective-permute-start(bf16[32,2304]{1,0:T(8,128)(2,1)S(1)} %collective-permute-done.10), channel_id=1, source_target_pairs={{0,4},{1,5},{2,6},{3,7},{4,64},{5,65},{6,66},{7,67},{8,12},{9,13},... | collective-permute-start | bytes 442376 | tf_op jit(solution)/shard_map/ppermute | solution.py:65
  60.7 12.8 %collective-permute-start.4 = (bf16[128,2176]{1,0:T(8,128)(2,1)S(1)}, bf16[128,2176]{1,0:T(8,128)(2,1)S(1)}, u32[]{:S(2)}, u32[]{:S(2)}) collective-permute-start(bf16[128,2176]{1,0:T(8,128)(2,1)S(1)} %pad_maximum_fusion.8), channel_id=1, source_target_pairs={{0,4},{1,5},{2,6},{3,7},{4,64},{5,65},{6,66},{7,67},{8,12},{9,13},... | collective-permute-start | bytes 1671176 | tf_op jit(solution)/shard_map/ppermute | solution.py:63
  60.8 16.0 %collective-permute-start.5 = (bf16[128,2176]{1,0:T(8,128)(2,1)S(1)}, bf16[128,2176]{1,0:T(8,128)(2,1)S(1)}, u32[]{:S(2)}, u32[]{:S(2)}) collective-permute-start(bf16[128,2176]{1,0:T(8,128)(2,1)S(1)} %pad_maximum_fusion.8), channel_id=1, source_target_pairs={{0,68},{1,69},{2,70},{3,71},{4,0},{5,1},{6,2},{7,3},{8,76},{9,77},... | collective-permute-start | bytes 1671176 | tf_op jit(solution)/shard_map/ppermute | solution.py:64
  64.8 14.3 %collective-permute-start.22 = (bf16[128,2304]{1,0:T(8,128)(2,1)S(1)}, bf16[128,2304]{1,0:T(8,128)(2,1)S(1)}, u32[]{:S(2)}, u32[]{:S(2)}) collective-permute-start(bf16[128,2304]{1,0:T(8,128)(2,1)S(1)} %pad_maximum_fusion.7), channel_id=1, source_target_pairs={{0,8},{1,9},{2,10},{3,11},{4,12},{5,13},{6,14},{7,15},{8,16},{9,17... | collective-permute-start | bytes 1769480 | tf_op jit(solution)/shard_map/ppermute | solution.py:63
  64.9 20.4 %collective-permute-start.23 = (bf16[128,2304]{1,0:T(8,128)(2,1)S(1)}, bf16[128,2304]{1,0:T(8,128)(2,1)S(1)}, u32[]{:S(2)}, u32[]{:S(2)}) collective-permute-start(bf16[128,2304]{1,0:T(8,128)(2,1)S(1)} %pad_maximum_fusion.7), channel_id=1, source_target_pairs={{0,24},{1,25},{2,26},{3,27},{4,28},{5,29},{6,30},{7,31},{8,0},{9,1... | collective-permute-start | bytes 1769480 | tf_op jit(solution)/shard_map/ppermute | solution.py:64
  68.2 14.6 %collective-permute-start.13 = (bf16[128,2304]{1,0:T(8,128)(2,1)S(1)}, bf16[128,2304]{1,0:T(8,128)(2,1)S(1)}, u32[]{:S(2)}, u32[]{:S(2)}) collective-permute-start(bf16[128,2304]{1,0:T(8,128)(2,1)S(1)} %pad_maximum_fusion.6), channel_id=1, source_target_pairs={{0,1},{1,2},{2,3},{3,0},{4,5},{5,6},{6,7},{7,4},{8,9},{9,10},{10,1... | collective-permute-start | bytes 1769480 | tf_op jit(solution)/shard_map/ppermute | solution.py:63
  73.5 17.5 %collective-permute-start.14 = (bf16[128,2304]{1,0:T(8,128)(2,1)S(1)}, bf16[128,2304]{1,0:T(8,128)(2,1)S(1)}, u32[]{:S(2)}, u32[]{:S(2)}) collective-permute-start(bf16[128,2304]{1,0:T(8,128)(2,1)S(1)} %pad_maximum_fusion.6), channel_id=1, source_target_pairs={{0,3},{1,0},{2,1},{3,2},{4,7},{5,4},{6,5},{7,6},{8,11},{9,8},{10,9... | collective-permute-start | bytes 1769480 | tf_op jit(solution)/shard_map/ppermute | solution.py:64
  76.8 13.1 %collective-permute-start.6 = (bf16[128,2176]{1,0:T(8,128)(2,1)S(1)}, bf16[128,2176]{1,0:T(8,128)(2,1)S(1)}, u32[]{:S(2)}, u32[]{:S(2)}) collective-permute-start(bf16[128,2176]{1,0:T(8,128)(2,1)S(1)} %collective-permute-done.4), channel_id=1, source_target_pairs={{0,4},{1,5},{2,6},{3,7},{4,64},{5,65},{6,66},{7,67},{8,12},{9,13},... | collective-permute-start | bytes 1671176 | tf_op jit(solution)/shard_map/ppermute | solution.py:65
  79.1 16.2 %collective-permute-start.24 = (bf16[128,2304]{1,0:T(8,128)(2,1)S(1)}, bf16[128,2304]{1,0:T(8,128)(2,1)S(1)}, u32[]{:S(2)}, u32[]{:S(2)}) collective-permute-start(bf16[128,2304]{1,0:T(8,128)(2,1)S(1)} %collective-permute-done.22), channel_id=1, source_target_pairs={{0,8},{1,9},{2,10},{3,11},{4,12},{5,13},{6,14},{7,15},{8,16},{9,17... | collective-permute-start | bytes 1769480 | tf_op jit(solution)/shard_map/ppermute | solution.py:65
  82.8 17.6 %collective-permute-start.15 = (bf16[128,2304]{1,0:T(8,128)(2,1)S(1)}, bf16[128,2304]{1,0:T(8,128)(2,1)S(1)}, u32[]{:S(2)}, u32[]{:S(2)}) collective-permute-start(bf16[128,2304]{1,0:T(8,128)(2,1)S(1)} %collective-permute-done.13), channel_id=1, source_target_pairs={{0,1},{1,2},{2,3},{3,0},{4,5},{5,6},{6,7},{7,4},{8,9},{9,10},{10,1... | collective-permute-start | bytes 1769480 | tf_op jit(solution)/shard_map/ppermute | solution.py:65
  85.3 17.9 %copy-start.13 = (s32[4]{0:T(128)S(1)}, s32[4]{0:T(128)}, u32[]{:S(2)}) copy-start(s32[4]{0:T(128)} %param.26) | copy-start | bytes 52
  85.3 18.9 %copy-start.11 = (bf16[4,64]{1,0:T(4,128)(2,1)S(1)}, bf16[4,64]{1,0:T(4,128)(2,1)}, u32[]{:S(2)}) copy-start(bf16[4,64]{1,0:T(4,128)(2,1)} %param.18) | copy-start | bytes 1540
  91.0 135.6 %collective-permute-start.7 = (bf16[512,2176]{1,0:T(8,128)(2,1)}, bf16[512,2176]{1,0:T(8,128)(2,1)}, u32[]{:S(2)}, u32[]{:S(2)}) collective-permute-start(bf16[512,2176]{1,0:T(8,128)(2,1)} %get-tuple-element.47), channel_id=1, source_target_pairs={{0,1},{1,2},{2,3},{3,0},{4,5},{5,6},{6,7},{7,4},{8,9},{9,10},{10,1... | collective-permute-start | bytes 6684680 | tf_op jit(solution)/shard_map/ppermute | solution.py:63
  92.1 137.7 %collective-permute-start.8 = (bf16[512,2176]{1,0:T(8,128)(2,1)}, bf16[512,2176]{1,0:T(8,128)(2,1)}, u32[]{:S(2)}, u32[]{:S(2)}) collective-permute-start(bf16[512,2176]{1,0:T(8,128)(2,1)} %get-tuple-element.47), channel_id=1, source_target_pairs={{0,3},{1,0},{2,1},{3,2},{4,7},{5,4},{6,5},{7,6},{8,11},{9,8},{10,9... | collective-permute-start | bytes 6684680 | tf_op jit(solution)/shard_map/ppermute | solution.py:64
  96.5 140.0 %collective-permute-start.25 = (bf16[512,2304]{1,0:T(8,128)(2,1)}, bf16[512,2304]{1,0:T(8,128)(2,1)S(1)}, u32[]{:S(2)}, u32[]{:S(2)}) collective-permute-start(bf16[512,2304]{1,0:T(8,128)(2,1)} %get-tuple-element.41), channel_id=1, source_target_pairs={{0,4},{1,5},{2,6},{3,7},{4,64},{5,65},{6,66},{7,67},{8,12},{9,13},... | collective-permute-start | bytes 7077896 | tf_op jit(solution)/shard_map/ppermute | solution.py:63
  101.5 135.0 %collective-permute-start.16 = (bf16[512,2304]{1,0:T(8,128)(2,1)}, bf16[512,2304]{1,0:T(8,128)(2,1)}, u32[]{:S(2)}, u32[]{:S(2)}) collective-permute-start(bf16[512,2304]{1,0:T(8,128)(2,1)} %get-tuple-element.35), channel_id=1, source_target_pairs={{0,8},{1,9},{2,10},{3,11},{4,12},{5,13},{6,14},{7,15},{8,16},{9,17... | collective-permute-start | bytes 7077896 | tf_op jit(solution)/shard_map/ppermute | solution.py:63
  103.2 140.2 %collective-permute-start.26 = (bf16[512,2304]{1,0:T(8,128)(2,1)}, bf16[512,2304]{1,0:T(8,128)(2,1)}, u32[]{:S(2)}, u32[]{:S(2)}) collective-permute-start(bf16[512,2304]{1,0:T(8,128)(2,1)} %get-tuple-element.41), channel_id=1, source_target_pairs={{0,68},{1,69},{2,70},{3,71},{4,0},{5,1},{6,2},{7,3},{8,76},{9,77},... | collective-permute-start | bytes 7077896 | tf_op jit(solution)/shard_map/ppermute | solution.py:64
  226.6 36.0 %collective-permute-start.17 = (bf16[512,2304]{1,0:T(8,128)(2,1)}, bf16[512,2304]{1,0:T(8,128)(2,1)}, u32[]{:S(2)}, u32[]{:S(2)}) collective-permute-start(bf16[512,2304]{1,0:T(8,128)(2,1)} %get-tuple-element.35), channel_id=1, source_target_pairs={{0,24},{1,25},{2,26},{3,27},{4,28},{5,29},{6,30},{7,31},{8,0},{9,1... | collective-permute-start | bytes 7077896 | tf_op jit(solution)/shard_map/ppermute | solution.py:64
  229.8 36.1 %collective-permute-start.9 = (bf16[512,2176]{1,0:T(8,128)(2,1)}, bf16[512,2176]{1,0:T(8,128)(2,1)S(1)}, u32[]{:S(2)}, u32[]{:S(2)}) collective-permute-start(bf16[512,2176]{1,0:T(8,128)(2,1)} %collective-permute-done.7), channel_id=1, source_target_pairs={{0,1},{1,2},{2,3},{3,0},{4,5},{5,6},{6,7},{7,4},{8,9},{9,10},{10,1... | collective-permute-start | bytes 6684680 | tf_op jit(solution)/shard_map/ppermute | solution.py:65
  236.5 59.1 %collective-permute-start.27 = (bf16[512,2304]{1,0:T(8,128)(2,1)S(1)}, bf16[512,2304]{1,0:T(8,128)(2,1)}, u32[]{:S(2)}, u32[]{:S(2)}) collective-permute-start(bf16[512,2304]{1,0:T(8,128)(2,1)S(1)} %collective-permute-done.25), channel_id=1, source_target_pairs={{0,4},{1,5},{2,6},{3,7},{4,64},{5,65},{6,66},{7,67},{8,12},{9,13},... | collective-permute-start | bytes 7077896 | tf_op jit(solution)/shard_map/ppermute | solution.py:65
  236.5 73.2 %collective-permute-start.18 = (bf16[512,2304]{1,0:T(8,128)(2,1)}, bf16[512,2304]{1,0:T(8,128)(2,1)}, u32[]{:S(2)}, u32[]{:S(2)}) collective-permute-start(bf16[512,2304]{1,0:T(8,128)(2,1)} %collective-permute-done.16), channel_id=1, source_target_pairs={{0,8},{1,9},{2,10},{3,11},{4,12},{5,13},{6,14},{7,15},{8,16},{9,17... | collective-permute-start | bytes 7077896 | tf_op jit(solution)/shard_map/ppermute | solution.py:65
  323.8 12.9 %copy-start.5 = (bf16[512,2048]{1,0:T(8,128)(2,1)S(1)}, bf16[512,2048]{1,0:T(8,128)(2,1)}, u32[]{:S(2)}) copy-start(bf16[512,2048]{1,0:T(8,128)(2,1)} %param.17) | copy-start | bytes 6291460
  323.8 12.9 %copy-start.14 = (f32[2048]{0:T(1024)S(1)}, f32[2048]{0:T(1024)}, u32[]{:S(2)}) copy-start(f32[2048]{0:T(1024)} %param.19) | copy-start | bytes 24580
  361.6 2.5 copy-start.9
  372.9 5.0 %slice-start = ((s8[4259840]{0:T(1024)(128)(4,1)}), s8[4194304]{0:T(1024)(128)(4,1)S(1)}, s32[]{:S(2)}) async-start(s8[4259840]{0:T(1024)(128)(4,1)} %bitcast.51), calls=%async_computation.2 | async-start | bytes 8388608
  372.9 5.0 %slice-start.1 = ((s8[4259840]{0:T(1024)(128)(4,1)}), s8[65536]{0:T(1024)(128)(4,1)S(1)}, s32[]{:S(2)}) async-start(s8[4259840]{0:T(1024)(128)(4,1)} %bitcast.51), calls=%async_computation.3 | async-start | bytes 131072
  378.0 3.4 copy-start.2
  379.4 2.6 copy-start.3
  379.4 3.2 copy-start.4
  418.0 35.4 %slice-start.2 = ((s8[8388608]{0:T(1024)(128)(4,1)}), s8[4194304]{0:T(1024)(128)(4,1)S(1)}, s32[]{:S(2)}) async-start(s8[8388608]{0:T(1024)(128)(4,1)} %bitcast.57), calls=%async_computation.4 | async-start | bytes 8388608
  436.1 10.2 %copy-start.6 = (bf16[512,16,128]{2,1,0:T(8,128)(2,1)S(1)}, bf16[512,16,128]{2,1,0:T(8,128)(2,1)}, u32[]{:S(2)}) copy-start(bf16[512,16,128]{2,1,0:T(8,128)(2,1)} %get-tuple-element.33) | copy-start | bytes 6291460
  436.1 10.2 %copy-start.8 = (bf16[4,16,512]{2,0,1:T(4,128)(2,1)S(1)}, bf16[4,16,512]{2,0,1:T(4,128)(2,1)}, u32[]{:S(2)}) copy-start(bf16[4,16,512]{2,0,1:T(4,128)(2,1)} %fusion.44) | copy-start | bytes 196612
  436.1 17.2 %slice-start.3 = ((s8[8388608]{0:T(1024)(128)(4,1)}), s8[4194304]{0:T(1024)(128)(4,1)S(1)}, s32[]{:S(2)}) async-start(s8[8388608]{0:T(1024)(128)(4,1)} %bitcast.57), calls=%async_computation.5 | async-start | bytes 8388608
  (1 other events, 1.5 us)
Sparse Core Ops, SparseCore 0:
  24.8 156.1 all-gather.2
